TPU v7x, 256 devices: a whole 4x4x8 slice. The times are simulated.
256 devices in a mesh: dp: 16 (over z_lo, x), tensor: 16 (over y, z_hi, core).
Axes of the slice: x: 4, y: 4, z: 8 (z_hi: 2, z_lo: 4; z = z_hi * 4 + z_lo), core: 2. Of those that a mesh axis runs over, the one named last changes fastest.
Arguments:
- inner_x: bfloat16 [16, 2048, 7168], P('dp', None, 'tensor')
- gate_z: bfloat16 [16, 2048, 7168], P('dp', None, 'tensor'), may hold values from -6 to 6
- input_b: bfloat16 [16, 2048, 128], P('dp'), may hold values from -0.75 to 0.75
- output_c: bfloat16 [16, 2048, 128], P('dp'), may hold values from -6 to 6
- step_raw: float32 [16, 2048, 112], P('dp', None, 'tensor'), may hold values from -6 to 6
- decay_rate: float32 [112], P('tensor'), may hold values from 0.001 to 0.05
- skip_gain: float32 [112], P('tensor'), may hold values from 0.5 to 1.5
- norm_gain: float32 [7168], P('tensor'), may hold values from 0.5 to 1.5
- out_weight: bfloat16 [7168, 3584], P('tensor'), may hold values from -0.0625 to 0.0625
- segment: int32 [16, 2048], P('dp'), may hold values from 0 to 7, never falling along the last dimension, each value on 1 to 1024 neighbouring positions
- cache_slot: int32 [16, 8], replicated, may hold values from 0 to 127, as said below
Outputs:
- mixed: bfloat16 [16, 2048, 3584], P('dp', 'tensor')
- cache: float32 [128, 112, 4096], P('dp', 'tensor')
Inputs may be any that keep to these rules, and one draw needn't show every extreme that they name: `segment`: in each group's row the prompt numbers never fall and every prompt 0 to 7 is present. `cache_slot`: every slot is named exactly once; slot // 8 is the owning group, and no two prompts of one group have the same owning group.
All inputs are finite; a program needn't handle non-finite values.
Results may differ from a plain program's by a relative error of at most 0.018.
Values may be sent and summed in bfloat16 or wider, within the bound.
No kernel may reach another device: no remote copies, remote signals or barrier semaphores. Data moves between devices by JAX's collectives and lax.ppermute only.
A program may use at most 192 MiB of HBM per device.

v0:
```python
import jax
import jax.numpy as jnp
from jax import lax
from jax.sharding import PartitionSpec as P

HEADS = 112
HEAD = 64
STATE = 64
NGROUPS = 2
REQS = 8
BLOCK = 256
INNER = 7168
HIGHEST = lax.Precision.HIGHEST


def split_pair(values):
    upper = values.astype(jnp.bfloat16)
    lower = (values - upper.astype(jnp.float32)).astype(jnp.bfloat16)
    return (upper, lower)


def split_einsum(form, wide, narrow):
    upper, lower = split_pair(wide)
    first = jnp.einsum(form, upper, narrow, preferred_element_type=jnp.float32)
    return first + jnp.einsum(form, lower, narrow, preferred_element_type=jnp.float32)


def local(
    inner_x,
    gate_z,
    input_b,
    output_c,
    step_raw,
    decay_rate,
    skip_gain,
    norm_gain,
    out_weight,
    segment,
    cache_slot,
):
    stream_len = inner_x.shape[1]
    dev_width = inner_x.shape[2]
    dev_heads = decay_rate.shape[0]
    tensor_idx = lax.axis_index("tensor")
    group_idx = tensor_idx * dev_heads // (HEADS // NGROUPS)
    b_cols = lax.dynamic_slice_in_dim(input_b[0], group_idx * STATE, STATE, 1)
    c_cols = lax.dynamic_slice_in_dim(output_c[0], group_idx * STATE, STATE, 1)
    step_size = jax.nn.softplus(step_raw[0])
    cum_log = jnp.cumsum(-decay_rate[None, :] * step_size, axis=0)
    seg_row = segment[0]
    block_count = stream_len // BLOCK
    prev_cum = jnp.concatenate([jnp.zeros((1, dev_heads), jnp.float32), cum_log[:-1]], axis=0)[
        ::BLOCK
    ]
    prev_seg = jnp.concatenate([jnp.full((1,), -1, seg_row.dtype), seg_row[:-1]], axis=0)[::BLOCK]
    block_inputs = (
        inner_x[0].reshape(block_count, BLOCK, dev_heads, HEAD),
        cum_log.reshape(block_count, BLOCK, dev_heads),
        step_size.reshape(block_count, BLOCK, dev_heads),
        seg_row.reshape(block_count, BLOCK),
        b_cols.reshape(block_count, BLOCK, STATE),
        c_cols.reshape(block_count, BLOCK, STATE),
        prev_cum,
        prev_seg,
    )
    positions = jnp.arange(BLOCK)

    def advance(carried, block_in):
        x_blk, cum_blk, step_blk, seg_blk, b_blk, c_blk, prev_c, prev_s = block_in
        scores = jnp.dot(c_blk, b_blk.T, preferred_element_type=jnp.float32)
        causal_mask = (positions[None, :] <= positions[:, None]) & (
            seg_blk[:, None] == seg_blk[None, :]
        )
        log_gap = cum_blk.T[:, :, None] - cum_blk.T[:, None, :]
        weights = (
            jnp.exp(jnp.where(causal_mask[None], log_gap, -jnp.inf))
            * step_blk.T[:, None, :]
            * scores[None]
        )
        intra_part = split_einsum("hts,shp->thp", weights, x_blk)
        live_rows = (seg_blk == prev_s).astype(jnp.float32)
        carry_decay = jnp.exp(cum_blk - prev_c[None, :]) * live_rows[:, None]
        carry_part = split_einsum("hpn,tn->thp", carried, c_blk) * carry_decay[:, :, None]
        outputs = intra_part + carry_part + skip_gain[None, :, None] * x_blk.astype(jnp.float32)
        last_seg = seg_blk[-1]
        last_cum = cum_blk[-1]
        keep_rows = (last_seg == prev_s).astype(jnp.float32)
        pull_back = (
            jnp.exp(last_cum[None, :] - cum_blk)
            * step_blk
            * (seg_blk == last_seg).astype(jnp.float32)[:, None]
        )
        added_part = split_einsum("shp,sn->hpn", pull_back[:, :, None] * x_blk, b_blk)
        carried = carried * (jnp.exp(last_cum - prev_c) * keep_rows)[:, None, None] + added_part
        return (carried, outputs)

    _, outputs = lax.scan(advance, jnp.zeros((dev_heads, HEAD, STATE), jnp.float32), block_inputs)
    mixer_y = outputs.reshape(stream_len, dev_width)
    members = (seg_row[None, :] == jnp.arange(REQS)[:, None]).astype(jnp.float32)
    end_index = (
        jnp.sum((seg_row[None, :] <= jnp.arange(REQS)[:, None]).astype(jnp.int32), axis=1) - 1
    )
    at_end = (jnp.arange(stream_len)[None, :] == end_index[:, None]).astype(jnp.float32)
    end_cum = jnp.dot(at_end, cum_log, precision=HIGHEST)
    seg_end_cum = jnp.dot(members.T, end_cum, precision=HIGHEST)
    pull_all = jnp.exp(seg_end_cum - cum_log) * step_size
    weighted = (inner_x[0].reshape(stream_len, dev_heads, HEAD) * pull_all[:, :, None]).reshape(
        stream_len, dev_width
    )
    masked_b = (
        (members.astype(jnp.bfloat16)[:, :, None] * b_cols[None])
        .transpose(1, 0, 2)
        .reshape(stream_len, REQS * STATE)
    )
    finals = split_einsum("tc,tk->ck", weighted, masked_b)
    finals = (
        finals.reshape(dev_heads, HEAD, REQS, STATE)
        .transpose(2, 0, 1, 3)
        .reshape(REQS, dev_heads * HEAD * STATE)
    )
    gated = mixer_y * jax.nn.silu(gate_z[0].astype(jnp.float32))
    sum_sq = jnp.sum(gated * gated, axis=1)
    group_hot = (jnp.arange(NGROUPS) == group_idx).astype(jnp.float32)
    group_stat = lax.psum(sum_sq[:, None] * group_hot[None, :], "tensor")
    mean_sq = jnp.sum(group_stat * group_hot[None, :], axis=1) / (INNER // NGROUPS)
    rounded = (gated * lax.rsqrt(mean_sq + 1e-05)[:, None] * norm_gain[None, :]).astype(
        jnp.bfloat16
    )
    projected = lax.psum_scatter(
        jnp.dot(rounded, out_weight, preferred_element_type=jnp.float32).astype(jnp.bfloat16),
        "tensor",
        scatter_dimension=0,
        tiled=True,
    )
    mixed = projected[None]
    dp_idx = lax.axis_index("dp")
    dp_size = lax.axis_size("dp")
    own_slots = lax.dynamic_slice_in_dim(cache_slot, dp_idx, 1, 0)[0]
    dest_hot = ((own_slots // REQS)[:, None] == jnp.arange(dp_size)[None, :]).astype(jnp.float32)
    outbound = jnp.dot(dest_hot.T, finals, precision=HIGHEST).reshape(
        dp_size, dev_heads, HEAD * STATE
    )
    inbound = lax.all_to_all(
        outbound.astype(jnp.bfloat16), "dp", split_axis=0, concat_axis=0, tiled=True
    ).astype(outbound.dtype)
    wanted = dp_idx * REQS + jnp.arange(REQS)
    take_hot = jnp.any(cache_slot[:, :, None] == wanted[None, None, :], axis=1).astype(jnp.float32)
    cache = jnp.dot(
        take_hot.T, inbound.reshape(dp_size, dev_heads * HEAD * STATE), precision=HIGHEST
    )
    return (mixed, cache.reshape(REQS, dev_heads, HEAD * STATE))


def solution(mesh):
    in_specs = (
        P("dp", None, "tensor"),
        P("dp", None, "tensor"),
        P("dp", None, None),
        P("dp", None, None),
        P("dp", None, "tensor"),
        P("tensor"),
        P("tensor"),
        P("tensor"),
        P("tensor", None),
        P("dp", None),
        P(),
    )
    out_specs = (P("dp", "tensor", None), P("dp", "tensor", None))
    return jax.shard_map(local, mesh=mesh, in_specs=in_specs, out_specs=out_specs, check_vma=False)
```

profile of v0, /device:TPU:32, one launch (start us, length us, event | category | flops | bytes accessed | tf_op | source)
XLA Modules:
  0.0 556.6 jit_solution(15308856619682689794)
XLA Ops:
  7.8 2.8 constant_dynamic-slice_fusion.3
  10.7 1.9 copy.77
  14.3 1.9 copy.65
  16.4 2.0 reduce-window.6
  21.2 2.1 copy.87
  23.3 1.7 copy.63
  25.0 1.6 reduce.4
  26.6 1.5 compare_select_fusion.1
  30.0 217.2 %while.13 = (s32[]{:T(128)}, f32[7,64,64]{2,1,0:T(8,128)S(1)}, f32[8,256,7,64]{1,0,3,2:T(8,128)}, f32[8,256,7]{1,2,0:T(8,128)S(1)}, f32[8,7]{1,0:T(8,128)S(1)}, ...) while((s32[]{:T(128)}, f32[7,64,64]{2,1,0:T(8,128)S(1)}, ...), condition=%wide.region_3.4_spmd.clone, body=%wide.region_2.3_spmd.clone.sunk | while | flops 192841488 | bytes 8220087 | solution.py:97
  30.7 1.3 dynamic_slice.129
  33.5 1.3 compare_convert_fusion.4
  38.8 1.6 fusion.151
  40.4 1.8 fusion.152
  43.5 11.3 %dynamic_update_slice.6 = f32[8,256,7,64]{1,0,3,2:T(8,128)} dynamic-update-slice(f32[8,256,7,64]{1,0,3,2:T(8,128)} %get-tuple-element.315, f32[1,256,7,64]{1,0,3,2:T(1,128)} %copy.140, s32[]{:T(128)} %get-tuple-element.313, s32[]{:T(128)} %constant.69.clone.1..sunk, s32[]{:T(128)} %constant.69.clone.1..sunk, s32[]{:T(128)} %constant.69.clone.1..sunk) | dynamic-update-slice | bytes 917508 | tf_op jit(solution)/shard_map/while/body/jit(dynamic_update_index_in_dim)/dynamic_update_slice | solution.py:97
  57.8 1.3 dynamic_slice.129
  60.7 1.3 compare_convert_fusion.4
  66.0 1.6 fusion.151
  67.6 1.8 fusion.152
  70.7 11.3 %dynamic_update_slice.6 = f32[8,256,7,64]{1,0,3,2:T(8,128)} dynamic-update-slice(f32[8,256,7,64]{1,0,3,2:T(8,128)} %get-tuple-element.315, f32[1,256,7,64]{1,0,3,2:T(1,128)} %copy.140, s32[]{:T(128)} %get-tuple-element.313, s32[]{:T(128)} %constant.69.clone.1..sunk, s32[]{:T(128)} %constant.69.clone.1..sunk, s32[]{:T(128)} %constant.69.clone.1..sunk) | dynamic-update-slice | bytes 917508 | tf_op jit(solution)/shard_map/while/body/jit(dynamic_update_index_in_dim)/dynamic_update_slice | solution.py:97
  85.0 1.3 dynamic_slice.129
  87.8 1.3 compare_convert_fusion.4
  93.1 1.6 fusion.151
  94.7 1.8 fusion.152
  97.8 11.3 %dynamic_update_slice.6 = f32[8,256,7,64]{1,0,3,2:T(8,128)} dynamic-update-slice(f32[8,256,7,64]{1,0,3,2:T(8,128)} %get-tuple-element.315, f32[1,256,7,64]{1,0,3,2:T(1,128)} %copy.140, s32[]{:T(128)} %get-tuple-element.313, s32[]{:T(128)} %constant.69.clone.1..sunk, s32[]{:T(128)} %constant.69.clone.1..sunk, s32[]{:T(128)} %constant.69.clone.1..sunk) | dynamic-update-slice | bytes 917508 | tf_op jit(solution)/shard_map/while/body/jit(dynamic_update_index_in_dim)/dynamic_update_slice | solution.py:97
  112.1 1.3 dynamic_slice.129
  115.0 1.3 compare_convert_fusion.4
  120.3 1.6 fusion.151
  121.9 1.8 fusion.152
  125.0 11.3 %dynamic_update_slice.6 = f32[8,256,7,64]{1,0,3,2:T(8,128)} dynamic-update-slice(f32[8,256,7,64]{1,0,3,2:T(8,128)} %get-tuple-element.315, f32[1,256,7,64]{1,0,3,2:T(1,128)} %copy.140, s32[]{:T(128)} %get-tuple-element.313, s32[]{:T(128)} %constant.69.clone.1..sunk, s32[]{:T(128)} %constant.69.clone.1..sunk, s32[]{:T(128)} %constant.69.clone.1..sunk) | dynamic-update-slice | bytes 917508 | tf_op jit(solution)/shard_map/while/body/jit(dynamic_update_index_in_dim)/dynamic_update_slice | solution.py:97
  139.3 1.3 dynamic_slice.129
  142.1 1.3 compare_convert_fusion.4
  147.4 1.6 fusion.151
  149.0 1.8 fusion.152
  152.1 11.3 %dynamic_update_slice.6 = f32[8,256,7,64]{1,0,3,2:T(8,128)} dynamic-update-slice(f32[8,256,7,64]{1,0,3,2:T(8,128)} %get-tuple-element.315, f32[1,256,7,64]{1,0,3,2:T(1,128)} %copy.140, s32[]{:T(128)} %get-tuple-element.313, s32[]{:T(128)} %constant.69.clone.1..sunk, s32[]{:T(128)} %constant.69.clone.1..sunk, s32[]{:T(128)} %constant.69.clone.1..sunk) | dynamic-update-slice | bytes 917508 | tf_op jit(solution)/shard_map/while/body/jit(dynamic_update_index_in_dim)/dynamic_update_slice | solution.py:97
  166.4 1.3 dynamic_slice.129
  169.3 1.3 compare_convert_fusion.4
  174.6 1.6 fusion.151
  176.2 1.8 fusion.152
  179.3 11.3 %dynamic_update_slice.6 = f32[8,256,7,64]{1,0,3,2:T(8,128)} dynamic-update-slice(f32[8,256,7,64]{1,0,3,2:T(8,128)} %get-tuple-element.315, f32[1,256,7,64]{1,0,3,2:T(1,128)} %copy.140, s32[]{:T(128)} %get-tuple-element.313, s32[]{:T(128)} %constant.69.clone.1..sunk, s32[]{:T(128)} %constant.69.clone.1..sunk, s32[]{:T(128)} %constant.69.clone.1..sunk) | dynamic-update-slice | bytes 917508 | tf_op jit(solution)/shard_map/while/body/jit(dynamic_update_index_in_dim)/dynamic_update_slice | solution.py:97
  193.6 1.3 dynamic_slice.129
  196.4 1.3 compare_convert_fusion.4
  201.7 1.6 fusion.151
  203.3 1.8 fusion.152
  206.4 11.3 %dynamic_update_slice.6 = f32[8,256,7,64]{1,0,3,2:T(8,128)} dynamic-update-slice(f32[8,256,7,64]{1,0,3,2:T(8,128)} %get-tuple-element.315, f32[1,256,7,64]{1,0,3,2:T(1,128)} %copy.140, s32[]{:T(128)} %get-tuple-element.313, s32[]{:T(128)} %constant.69.clone.1..sunk, s32[]{:T(128)} %constant.69.clone.1..sunk, s32[]{:T(128)} %constant.69.clone.1..sunk) | dynamic-update-slice | bytes 917508 | tf_op jit(solution)/shard_map/while/body/jit(dynamic_update_index_in_dim)/dynamic_update_slice | solution.py:97
  220.7 1.3 dynamic_slice.129
  223.6 1.3 compare_convert_fusion.4
  228.9 1.6 fusion.151
  230.5 1.8 fusion.152
  233.6 11.3 %dynamic_update_slice.6 = f32[8,256,7,64]{1,0,3,2:T(8,128)} dynamic-update-slice(f32[8,256,7,64]{1,0,3,2:T(8,128)} %get-tuple-element.315, f32[1,256,7,64]{1,0,3,2:T(1,128)} %copy.140, s32[]{:T(128)} %get-tuple-element.313, s32[]{:T(128)} %constant.69.clone.1..sunk, s32[]{:T(128)} %constant.69.clone.1..sunk, s32[]{:T(128)} %constant.69.clone.1..sunk) | dynamic-update-slice | bytes 917508 | tf_op jit(solution)/shard_map/while/body/jit(dynamic_update_index_in_dim)/dynamic_update_slice | solution.py:97
  247.2 1.9 convert_element_type.191
  249.1 1.7 copy.90
  252.5 92.2 %psum.7 = f32[2048,2]{0,1:T(2,128)S(1)} all-reduce(f32[2048,2]{0,1:T(2,128)S(1)} %broadcast_multiply_fusion.1), channel_id=1, replica_groups=mesh['dp'=16,'tensor'=16] {'tensor'}, use_global_device_ids=true, to_apply=%region_5.6 | all-reduce | flops 4096 | bytes 32768 | tf_op jit(solution)/shard_map/psum | solution.py:124
  344.8 3.9 copy.89
  348.7 11.6 %convolution_convert_fusion = bf16[2048,3584]{1,0:T(8,128)(2,1)} fusion(bf16[448,3584]{1,0:T(8,128)(2,1)S(1)} %copy-done, f32[2048,448]{0,1:T(8,128)S(1)} %bitcast.258, f32[448]{0:T(512)S(1)} %copy-done.13, f32[2048]{0:T(1024)S(1)} %add_rsqrt_fusion, bf16[1,2048,448]{1,2,0:T(8,128)(2,1)S(1)} %copy-done.4), kind=kOutput, calls=%fused_computation.84 | convolution fusion | flops 6592266240 | bytes 23406336 | tf_op jit(solution)/shard_map/dot_general | solution.py:130
  364.6 2.1 convolution_add_fusion.3
  366.7 2.7 reshape.350
  369.4 3.4 copy.134
  372.8 3.3 reshape.351
  376.3 2.3 convolution_convert_fusion.1
  378.6 1.5 copy.69
  380.1 6.6 %all-to-all-start = ((bf16[16,7,4096]{2,1,0:T(8,128)(2,1)}), bf16[16,7,4096]{2,1,0:T(8,128)(2,1)}, u32[]{:S(2)}, u32[]{:S(2)}) async-start(bf16[16,7,4096]{2,1,0:T(8,128)(2,1)} %copy.69), calls=%async_computation.1 | async-start | bytes 2097152 | tf_op jit(solution)/shard_map/all_to_all | solution.py:143
  386.7 17.7 %all-to-all-done = bf16[16,7,4096]{2,1,0:T(8,128)(2,1)} async-done(((bf16[16,7,4096]{2,1,0:T(8,128)(2,1)}), bf16[16,7,4096]{2,1,0:T(8,128)(2,1)}, u32[]{:S(2)}, u32[]{:S(2)}) %all-to-all-start) | async-done | bytes 917536 | tf_op jit(solution)/shard_map/all_to_all | solution.py:143
  404.5 3.2 fusion.83
  407.7 142.0 %reduce-scatter.2.cloned.1.call-done = bf16[128,3584]{1,0:T(8,128)(2,1)} async-done(((bf16[2048,3584]{1,0:T(8,128)(2,1)}), bf16[128,3584]{1,0:T(8,128)(2,1)}) %reduce-scatter.2.cloned.1.call-update) | async-done | bytes 917520 | tf_op jit(solution)/shard_map/reduce_scatter | solution.py:129
  (225 shorter events, 80.1 us)
Async XLA Ops:
  7.2 341.5 %copy-start = (bf16[448,3584]{1,0:T(8,128)(2,1)S(1)}, bf16[448,3584]{1,0:T(8,128)(2,1)}, u32[]{:S(2)}) copy-start(bf16[448,3584]{1,0:T(8,128)(2,1)} %param.21) | copy-start | bytes 9633796
  7.2 542.6 %reduce-scatter.2.cloned.1.call-start = ((), (), s32[]{:S(2)}) async-start(), calls=%async_computation.2 | async-start | bytes 15597568 | tf_op jit(solution)/shard_map/reduce_scatter | solution.py:129
  7.8 8.5 %copy-start.14 = (f32[7]{0:T(128)S(1)}, f32[7]{0:T(128)}, u32[]{:S(2)}) copy-start(f32[7]{0:T(128)} %param.18) | copy-start | bytes 88
  7.8 8.5 %copy-start.7 = (f32[1,2048,7]{1,0,2:T(1,128)S(1)}, f32[1,2048,7]{1,0,2:T(1,128)}, u32[]{:S(2)}) copy-start(f32[1,2048,7]{1,0,2:T(1,128)} %param.17) | copy-start | bytes 172036
  18.8 0.6 copy-start.5
  23.3 5.3 copy-start.8
  30.0 3.5 copy-start.10
  36.7 3.7 copy-start.15
  42.3 14.9 %copy-start.11 = (f32[8,7]{1,0:T(8,128)S(1)}, f32[8,7]{1,0:T(8,128)}, u32[]{:S(2)}) copy-start(f32[8,7]{1,0:T(8,128)} %copy-done.10) | copy-start | bytes 676 | tf_op jit(solution)/shard_map/while
  57.1 3.5 copy-start.10
  63.9 3.7 copy-start.15
  69.4 14.9 %copy-start.11 = (f32[8,7]{1,0:T(8,128)S(1)}, f32[8,7]{1,0:T(8,128)}, u32[]{:S(2)}) copy-start(f32[8,7]{1,0:T(8,128)} %copy-done.10) | copy-start | bytes 676 | tf_op jit(solution)/shard_map/while
  84.3 3.5 copy-start.10
  91.0 3.7 copy-start.15
  96.6 14.9 %copy-start.11 = (f32[8,7]{1,0:T(8,128)S(1)}, f32[8,7]{1,0:T(8,128)}, u32[]{:S(2)}) copy-start(f32[8,7]{1,0:T(8,128)} %copy-done.10) | copy-start | bytes 676 | tf_op jit(solution)/shard_map/while
  111.4 3.5 copy-start.10
  118.2 3.7 copy-start.15
  123.7 14.9 %copy-start.11 = (f32[8,7]{1,0:T(8,128)S(1)}, f32[8,7]{1,0:T(8,128)}, u32[]{:S(2)}) copy-start(f32[8,7]{1,0:T(8,128)} %copy-done.10) | copy-start | bytes 676 | tf_op jit(solution)/shard_map/while
  138.6 3.5 copy-start.10
  145.3 3.7 copy-start.15
  150.9 14.9 %copy-start.11 = (f32[8,7]{1,0:T(8,128)S(1)}, f32[8,7]{1,0:T(8,128)}, u32[]{:S(2)}) copy-start(f32[8,7]{1,0:T(8,128)} %copy-done.10) | copy-start | bytes 676 | tf_op jit(solution)/shard_map/while
  165.7 3.5 copy-start.10
  172.5 3.7 copy-start.15
  178.0 14.9 %copy-start.11 = (f32[8,7]{1,0:T(8,128)S(1)}, f32[8,7]{1,0:T(8,128)}, u32[]{:S(2)}) copy-start(f32[8,7]{1,0:T(8,128)} %copy-done.10) | copy-start | bytes 676 | tf_op jit(solution)/shard_map/while
  192.9 3.5 copy-start.10
  199.6 3.7 copy-start.15
  205.2 14.9 %copy-start.11 = (f32[8,7]{1,0:T(8,128)S(1)}, f32[8,7]{1,0:T(8,128)}, u32[]{:S(2)}) copy-start(f32[8,7]{1,0:T(8,128)} %copy-done.10) | copy-start | bytes 676 | tf_op jit(solution)/shard_map/while
  220.0 3.5 copy-start.10
  226.8 3.7 copy-start.15
  232.3 14.9 %copy-start.11 = (f32[8,7]{1,0:T(8,128)S(1)}, f32[8,7]{1,0:T(8,128)}, u32[]{:S(2)}) copy-start(f32[8,7]{1,0:T(8,128)} %copy-done.10) | copy-start | bytes 676 | tf_op jit(solution)/shard_map/while
  249.1 2.0 copy-start.1
  251.2 1.3 copy-start.12
  344.8 3.9 copy-start.4
  344.8 3.9 copy-start.13
  360.4 0.8 copy-start.6
  360.4 2.1 copy-start.3
  360.4 2.3 copy-start.2
  372.8 3.3 copy-start.9
  380.1 24.4 %all-to-all-start = ((bf16[16,7,4096]{2,1,0:T(8,128)(2,1)}), bf16[16,7,4096]{2,1,0:T(8,128)(2,1)}, u32[]{:S(2)}, u32[]{:S(2)}) async-start(bf16[16,7,4096]{2,1,0:T(8,128)(2,1)} %copy.69), calls=%async_computation.1 | async-start | bytes 2097152 | tf_op jit(solution)/shard_map/all_to_all | solution.py:143
Sparse Core Ops, SparseCore 0:
  360.5 189.1 reduce-scatter.1
where the time goes:
time: 562 us; the launch traced here: 557 us
  waiting for transfers between devices  160 us (28%)
  local copies, waits for them, and re-layouts  158 us (28%)
  blocking collectives  92.2 us (16%)
  matrix products  90.4 us (16%)
  other arithmetic  23.5 us (4%)
  between operations  14.3 us (3%)
  loops' own time  11.8 us (2%)
  starting transfers between devices  6.61 us (1%)
    reduce_scatter x1, waiting for transfers between devices, local(): lax.psum_scatter(jnp.dot(rounded, out_weight, preferred_element_type=jnp....  142 us
    dynamic_update_slice x16, local copies, waits for them, and re-layouts, local(): lax.scan(advance, jnp.zeros((dev_heads, HEAD, STATE), jnp.float32), block...  100 us
    psum x1, blocking collectives, local(): group_stat = lax.psum(sum_sq[:, None] * group_hot[None, :], 'tensor')  92.2 us
    dot_general x25, matrix products, split_einsum(): jnp.einsum(form, lower, narrow, preferred_element_type=jnp.float32)  33.6 us
    dot_general x25, matrix products, split_einsum(): first = jnp.einsum(form, upper, narrow, preferred_element_type=jnp.float32)  30.6 us
    all_to_all x1, waiting for transfers between devices, local(): lax.all_to_all(outbound.astype(jnp.bfloat16), 'dp', split_axis=0, concat_...  17.7 us
    unnamed x39, local copies, waits for them, and re-layouts  17.2 us
    dynamic_slice x24, local copies, waits for them, and re-layouts, local(): lax.scan(advance, jnp.zeros((dev_heads, HEAD, STATE), jnp.float32), block...  16.8 us
  transfers between devices with their start and end apart: 2, of which 2 were waited for; matrix products, arithmetic and copies ran while one was open for 4% of the time, Pallas kernels for 0%

commit v1 on v0

--- a/solution.py
+++ b/solution.py
@@ -121,7 +121,7 @@
     gated = mixer_y * jax.nn.silu(gate_z[0].astype(jnp.float32))
     sum_sq = jnp.sum(gated * gated, axis=1)
     group_hot = (jnp.arange(NGROUPS) == group_idx).astype(jnp.float32)
-    group_stat = lax.psum(sum_sq[:, None] * group_hot[None, :], "tensor")
+    group_stat = jnp.sum(lax.all_gather(sum_sq[:, None] * group_hot[None, :], "tensor"), axis=0)
     mean_sq = jnp.sum(group_stat * group_hot[None, :], axis=1) / (INNER // NGROUPS)
     rounded = (gated * lax.rsqrt(mean_sq + 1e-05)[:, None] * norm_gain[None, :]).astype(
         jnp.bfloat16

time: 562 us -> 505 us (0.90)
  blocking collectives: 92.2 us -> 35 us
    psum x1 -> x0, blocking collectives: 92.2 us -> none  [local(): group_stat = lax.psum(sum_sq[:, None] * group_hot[None, :], 'tensor')]
    reduce_scatter x1, waiting for transfers between devices: 142 us -> 72.5 us  [local(): lax.psum_scatter(jnp.dot(rounded, out_weight, preferred_element_type=jnp....]
    all_to_all x1, waiting for transfers between devices: 17.7 us -> 85.4 us  [local(): lax.all_to_all(outbound.astype(jnp.bfloat16), 'dp', split_axis=0, concat_...]
    all_gather x0 -> x1, blocking collectives: none -> 35 us  [local(): lax.all_gather(sum_sq[:, None] * group_hot[None, :], 'tensor')]
where the time goes in v1:
time: 505 us; the launch traced here: 499 us
  local copies, waits for them, and re-layouts  158 us (31%)
  waiting for transfers between devices  158 us (31%)
  matrix products  89.8 us (18%)
  blocking collectives  35 us (7%)
  other arithmetic  25.5 us (5%)
  between operations  14.3 us (3%)
  loops' own time  11.8 us (2%)
  starting transfers between devices  6.69 us (1%)
    dynamic_update_slice x16, local copies, waits for them, and re-layouts, local(): lax.scan(advance, jnp.zeros((dev_heads, HEAD, STATE), jnp.float32), block...  100 us
    all_to_all x1, waiting for transfers between devices, local(): lax.all_to_all(outbound.astype(jnp.bfloat16), 'dp', split_axis=0, concat_...  85.4 us
    reduce_scatter x1, waiting for transfers between devices, local(): lax.psum_scatter(jnp.dot(rounded, out_weight, preferred_element_type=jnp....  72.5 us
    all_gather x1, blocking collectives, local(): lax.all_gather(sum_sq[:, None] * group_hot[None, :], 'tensor')  35 us
    dot_general x25, matrix products, split_einsum(): jnp.einsum(form, lower, narrow, preferred_element_type=jnp.float32)  33.6 us
    dot_general x25, matrix products, split_einsum(): first = jnp.einsum(form, upper, narrow, preferred_element_type=jnp.float32)  30.6 us
    unnamed x39, local copies, waits for them, and re-layouts  17.2 us
    dynamic_slice x24, local copies, waits for them, and re-layouts, local(): lax.scan(advance, jnp.zeros((dev_heads, HEAD, STATE), jnp.float32), block...  16.8 us
  transfers between devices with their start and end apart: 2, of which 2 were waited for; matrix products, arithmetic and copies ran while one was open for 4% of the time, Pallas kernels for 0%

profile of v1, /device:TPU:32, one launch (start us, length us, event | category | flops | bytes accessed | tf_op | source)
XLA Modules:
  0.0 499.0 jit_solution(18085652721575162115)
XLA Ops:
  7.8 2.8 constant_dynamic-slice_fusion.3
  10.7 1.9 copy.91
  14.3 1.9 copy.79
  16.4 2.0 reduce-window.6
  21.2 2.1 copy.102
  23.3 1.7 copy.77
  25.0 1.6 reduce.4
  26.6 1.5 compare_select_fusion.1
  30.0 217.2 %while.13 = (s32[]{:T(128)}, f32[7,64,64]{2,1,0:T(8,128)S(1)}, f32[8,256,7,64]{1,0,3,2:T(8,128)}, f32[8,256,7]{1,2,0:T(8,128)S(1)}, f32[8,7]{1,0:T(8,128)S(1)}, ...) while((s32[]{:T(128)}, f32[7,64,64]{2,1,0:T(8,128)S(1)}, ...), condition=%wide.region_3.4_spmd.clone, body=%wide.region_2.3_spmd.clone.sunk | while | flops 192841488 | bytes 8220087 | solution.py:97
  30.7 1.3 dynamic_slice.129
  33.5 1.3 compare_convert_fusion.4
  38.8 1.6 fusion.151
  40.4 1.8 fusion.152
  43.5 11.3 %dynamic_update_slice.6 = f32[8,256,7,64]{1,0,3,2:T(8,128)} dynamic-update-slice(f32[8,256,7,64]{1,0,3,2:T(8,128)} %get-tuple-element.327, f32[1,256,7,64]{1,0,3,2:T(1,128)} %copy.155, s32[]{:T(128)} %get-tuple-element.325, s32[]{:T(128)} %constant.69.clone.1..sunk, s32[]{:T(128)} %constant.69.clone.1..sunk, s32[]{:T(128)} %constant.69.clone.1..sunk) | dynamic-update-slice | bytes 917508 | tf_op jit(solution)/shard_map/while/body/jit(dynamic_update_index_in_dim)/dynamic_update_slice | solution.py:97
  57.8 1.3 dynamic_slice.129
  60.7 1.3 compare_convert_fusion.4
  66.0 1.6 fusion.151
  67.6 1.8 fusion.152
  70.7 11.3 %dynamic_update_slice.6 = f32[8,256,7,64]{1,0,3,2:T(8,128)} dynamic-update-slice(f32[8,256,7,64]{1,0,3,2:T(8,128)} %get-tuple-element.327, f32[1,256,7,64]{1,0,3,2:T(1,128)} %copy.155, s32[]{:T(128)} %get-tuple-element.325, s32[]{:T(128)} %constant.69.clone.1..sunk, s32[]{:T(128)} %constant.69.clone.1..sunk, s32[]{:T(128)} %constant.69.clone.1..sunk) | dynamic-update-slice | bytes 917508 | tf_op jit(solution)/shard_map/while/body/jit(dynamic_update_index_in_dim)/dynamic_update_slice | solution.py:97
  85.0 1.3 dynamic_slice.129
  87.8 1.3 compare_convert_fusion.4
  93.1 1.6 fusion.151
  94.7 1.8 fusion.152
  97.8 11.3 %dynamic_update_slice.6 = f32[8,256,7,64]{1,0,3,2:T(8,128)} dynamic-update-slice(f32[8,256,7,64]{1,0,3,2:T(8,128)} %get-tuple-element.327, f32[1,256,7,64]{1,0,3,2:T(1,128)} %copy.155, s32[]{:T(128)} %get-tuple-element.325, s32[]{:T(128)} %constant.69.clone.1..sunk, s32[]{:T(128)} %constant.69.clone.1..sunk, s32[]{:T(128)} %constant.69.clone.1..sunk) | dynamic-update-slice | bytes 917508 | tf_op jit(solution)/shard_map/while/body/jit(dynamic_update_index_in_dim)/dynamic_update_slice | solution.py:97
  112.1 1.3 dynamic_slice.129
  115.0 1.3 compare_convert_fusion.4
  120.3 1.6 fusion.151
  121.9 1.8 fusion.152
  125.0 11.3 %dynamic_update_slice.6 = f32[8,256,7,64]{1,0,3,2:T(8,128)} dynamic-update-slice(f32[8,256,7,64]{1,0,3,2:T(8,128)} %get-tuple-element.327, f32[1,256,7,64]{1,0,3,2:T(1,128)} %copy.155, s32[]{:T(128)} %get-tuple-element.325, s32[]{:T(128)} %constant.69.clone.1..sunk, s32[]{:T(128)} %constant.69.clone.1..sunk, s32[]{:T(128)} %constant.69.clone.1..sunk) | dynamic-update-slice | bytes 917508 | tf_op jit(solution)/shard_map/while/body/jit(dynamic_update_index_in_dim)/dynamic_update_slice | solution.py:97
  139.3 1.3 dynamic_slice.129
  142.1 1.3 compare_convert_fusion.4
  147.4 1.6 fusion.151
  149.0 1.8 fusion.152
  152.1 11.3 %dynamic_update_slice.6 = f32[8,256,7,64]{1,0,3,2:T(8,128)} dynamic-update-slice(f32[8,256,7,64]{1,0,3,2:T(8,128)} %get-tuple-element.327, f32[1,256,7,64]{1,0,3,2:T(1,128)} %copy.155, s32[]{:T(128)} %get-tuple-element.325, s32[]{:T(128)} %constant.69.clone.1..sunk, s32[]{:T(128)} %constant.69.clone.1..sunk, s32[]{:T(128)} %constant.69.clone.1..sunk) | dynamic-update-slice | bytes 917508 | tf_op jit(solution)/shard_map/while/body/jit(dynamic_update_index_in_dim)/dynamic_update_slice | solution.py:97
  166.4 1.3 dynamic_slice.129
  169.3 1.3 compare_convert_fusion.4
  174.6 1.6 fusion.151
  176.2 1.8 fusion.152
  179.3 11.3 %dynamic_update_slice.6 = f32[8,256,7,64]{1,0,3,2:T(8,128)} dynamic-update-slice(f32[8,256,7,64]{1,0,3,2:T(8,128)} %get-tuple-element.327, f32[1,256,7,64]{1,0,3,2:T(1,128)} %copy.155, s32[]{:T(128)} %get-tuple-element.325, s32[]{:T(128)} %constant.69.clone.1..sunk, s32[]{:T(128)} %constant.69.clone.1..sunk, s32[]{:T(128)} %constant.69.clone.1..sunk) | dynamic-update-slice | bytes 917508 | tf_op jit(solution)/shard_map/while/body/jit(dynamic_update_index_in_dim)/dynamic_update_slice | solution.py:97
  193.6 1.3 dynamic_slice.129
  196.4 1.3 compare_convert_fusion.4
  201.7 1.6 fusion.151
  203.3 1.8 fusion.152
  206.4 11.3 %dynamic_update_slice.6 = f32[8,256,7,64]{1,0,3,2:T(8,128)} dynamic-update-slice(f32[8,256,7,64]{1,0,3,2:T(8,128)} %get-tuple-element.327, f32[1,256,7,64]{1,0,3,2:T(1,128)} %copy.155, s32[]{:T(128)} %get-tuple-element.325, s32[]{:T(128)} %constant.69.clone.1..sunk, s32[]{:T(128)} %constant.69.clone.1..sunk, s32[]{:T(128)} %constant.69.clone.1..sunk) | dynamic-update-slice | bytes 917508 | tf_op jit(solution)/shard_map/while/body/jit(dynamic_update_index_in_dim)/dynamic_update_slice | solution.py:97
  220.7 1.3 dynamic_slice.129
  223.6 1.3 compare_convert_fusion.4
  228.9 1.6 fusion.151
  230.5 1.8 fusion.152
  233.6 11.3 %dynamic_update_slice.6 = f32[8,256,7,64]{1,0,3,2:T(8,128)} dynamic-update-slice(f32[8,256,7,64]{1,0,3,2:T(8,128)} %get-tuple-element.327, f32[1,256,7,64]{1,0,3,2:T(1,128)} %copy.155, s32[]{:T(128)} %get-tuple-element.325, s32[]{:T(128)} %constant.69.clone.1..sunk, s32[]{:T(128)} %constant.69.clone.1..sunk, s32[]{:T(128)} %constant.69.clone.1..sunk) | dynamic-update-slice | bytes 917508 | tf_op jit(solution)/shard_map/while/body/jit(dynamic_update_index_in_dim)/dynamic_update_slice | solution.py:97
  247.2 1.9 convert_element_type.191
  249.1 1.7 copy.105
  252.5 35.0 %all_gather.4 = f32[16,2048,2]{1,2,0:T(2,128)} all-gather(f32[1,2048,2]{1,2,0:T(2,128)S(1)} %broadcast_multiply_fusion.1), channel_id=1, replica_groups=mesh['dp'=16,'tensor'=16] {'tensor'}, dimensions={0}, use_global_device_ids=true | all-gather | bytes 278528 | tf_op jit(solution)/shard_map/all_gather | solution.py:124
  288.7 3.9 copy.104
  292.6 11.8 %convolution_convert_fusion = bf16[2048,3584]{1,0:T(8,128)(2,1)} fusion(bf16[448,3584]{1,0:T(8,128)(2,1)S(1)} %copy-done, f32[2048,448]{0,1:T(8,128)S(1)} %bitcast.258, f32[448]{0:T(512)S(1)} %copy-done.13, f32[2048]{0:T(1024)S(1)} %add_rsqrt_fusion, bf16[1,2048,448]{1,2,0:T(8,128)(2,1)S(1)} %copy-done.3), kind=kOutput, calls=%fused_computation.84 | convolution fusion | flops 6592266240 | bytes 23406336 | tf_op jit(solution)/shard_map/dot_general | solution.py:130
  308.8 2.1 convolution_add_fusion.3
  310.9 2.7 reshape.402
  313.5 3.5 copy.149
  317.0 3.3 reshape.403
  320.5 2.3 convolution_convert_fusion.1
  322.8 1.5 copy.83
  324.3 6.7 %all-to-all-start = ((bf16[16,7,4096]{2,1,0:T(8,128)(2,1)}), bf16[16,7,4096]{2,1,0:T(8,128)(2,1)}, u32[]{:S(2)}, u32[]{:S(2)}) async-start(bf16[16,7,4096]{2,1,0:T(8,128)(2,1)} %copy.83), calls=%async_computation.1 | async-start | bytes 2097152 | tf_op jit(solution)/shard_map/all_to_all | solution.py:143
  331.0 85.4 %all-to-all-done = bf16[16,7,4096]{2,1,0:T(8,128)(2,1)} async-done(((bf16[16,7,4096]{2,1,0:T(8,128)(2,1)}), bf16[16,7,4096]{2,1,0:T(8,128)(2,1)}, u32[]{:S(2)}, u32[]{:S(2)}) %all-to-all-start) | async-done | bytes 917536 | tf_op jit(solution)/shard_map/all_to_all | solution.py:143
  416.4 3.2 fusion.83
  419.7 72.5 %reduce-scatter.2.cloned.1.call-done = bf16[128,3584]{1,0:T(8,128)(2,1)} async-done(((bf16[2048,3584]{1,0:T(8,128)(2,1)}), bf16[128,3584]{1,0:T(8,128)(2,1)}) %reduce-scatter.2.cloned.1.call-update) | async-done | bytes 917520 | tf_op jit(solution)/shard_map/reduce_scatter | solution.py:129
  (226 shorter events, 81.3 us)
Async XLA Ops:
  7.2 285.4 %copy-start = (bf16[448,3584]{1,0:T(8,128)(2,1)S(1)}, bf16[448,3584]{1,0:T(8,128)(2,1)}, u32[]{:S(2)}) copy-start(bf16[448,3584]{1,0:T(8,128)(2,1)} %param.21) | copy-start | bytes 9633796
  7.2 485.0 %reduce-scatter.2.cloned.1.call-start = ((), (), s32[]{:S(2)}) async-start(), calls=%async_computation.2 | async-start | bytes 15597568 | tf_op jit(solution)/shard_map/reduce_scatter | solution.py:129
  7.8 8.5 %copy-start.14 = (f32[7]{0:T(128)S(1)}, f32[7]{0:T(128)}, u32[]{:S(2)}) copy-start(f32[7]{0:T(128)} %param.18) | copy-start | bytes 88
  7.8 8.5 %copy-start.6 = (f32[1,2048,7]{1,0,2:T(1,128)S(1)}, f32[1,2048,7]{1,0,2:T(1,128)}, u32[]{:S(2)}) copy-start(f32[1,2048,7]{1,0,2:T(1,128)} %param.17) | copy-start | bytes 172036
  18.8 0.6 copy-start.4
  23.3 5.3 %copy-start.8 = (s32[1,2048]{1,0:T(1,128)S(1)}, s32[1,2048]{1,0:T(1,128)}, u32[]{:S(2)}) copy-start(s32[1,2048]{1,0:T(1,128)} %param.22) | copy-start | bytes 24580
  30.0 3.5 copy-start.10
  36.7 3.7 copy-start.15
  42.3 14.9 %copy-start.11 = (f32[8,7]{1,0:T(8,128)S(1)}, f32[8,7]{1,0:T(8,128)}, u32[]{:S(2)}) copy-start(f32[8,7]{1,0:T(8,128)} %copy-done.10) | copy-start | bytes 676 | tf_op jit(solution)/shard_map/while
  57.1 3.5 copy-start.10
  63.9 3.7 copy-start.15
  69.4 14.9 %copy-start.11 = (f32[8,7]{1,0:T(8,128)S(1)}, f32[8,7]{1,0:T(8,128)}, u32[]{:S(2)}) copy-start(f32[8,7]{1,0:T(8,128)} %copy-done.10) | copy-start | bytes 676 | tf_op jit(solution)/shard_map/while
  84.3 3.5 copy-start.10
  91.0 3.7 copy-start.15
  96.6 14.9 %copy-start.11 = (f32[8,7]{1,0:T(8,128)S(1)}, f32[8,7]{1,0:T(8,128)}, u32[]{:S(2)}) copy-start(f32[8,7]{1,0:T(8,128)} %copy-done.10) | copy-start | bytes 676 | tf_op jit(solution)/shard_map/while
  111.4 3.5 copy-start.10
  118.2 3.7 copy-start.15
  123.7 14.9 %copy-start.11 = (f32[8,7]{1,0:T(8,128)S(1)}, f32[8,7]{1,0:T(8,128)}, u32[]{:S(2)}) copy-start(f32[8,7]{1,0:T(8,128)} %copy-done.10) | copy-start | bytes 676 | tf_op jit(solution)/shard_map/while
  138.6 3.5 copy-start.10
  145.3 3.7 copy-start.15
  150.9 14.9 %copy-start.11 = (f32[8,7]{1,0:T(8,128)S(1)}, f32[8,7]{1,0:T(8,128)}, u32[]{:S(2)}) copy-start(f32[8,7]{1,0:T(8,128)} %copy-done.10) | copy-start | bytes 676 | tf_op jit(solution)/shard_map/while
  165.7 3.5 copy-start.10
  172.5 3.7 copy-start.15
  178.0 14.9 %copy-start.11 = (f32[8,7]{1,0:T(8,128)S(1)}, f32[8,7]{1,0:T(8,128)}, u32[]{:S(2)}) copy-start(f32[8,7]{1,0:T(8,128)} %copy-done.10) | copy-start | bytes 676 | tf_op jit(solution)/shard_map/while
  192.9 3.5 copy-start.10
  199.6 3.7 copy-start.15
  205.2 14.9 %copy-start.11 = (f32[8,7]{1,0:T(8,128)S(1)}, f32[8,7]{1,0:T(8,128)}, u32[]{:S(2)}) copy-start(f32[8,7]{1,0:T(8,128)} %copy-done.10) | copy-start | bytes 676 | tf_op jit(solution)/shard_map/while
  220.0 3.5 copy-start.10
  226.8 3.7 copy-start.15
  232.3 14.9 %copy-start.11 = (f32[8,7]{1,0:T(8,128)S(1)}, f32[8,7]{1,0:T(8,128)}, u32[]{:S(2)}) copy-start(f32[8,7]{1,0:T(8,128)} %copy-done.10) | copy-start | bytes 676 | tf_op jit(solution)/shard_map/while
  249.1 2.0 copy-start.1
  251.2 1.3 copy-start.12
  288.7 3.9 copy-start.3
  288.7 3.9 copy-start.13
  304.4 0.8 copy-start.5
  304.4 1.0 copy-start.7
  304.5 2.4 copy-start.2
  317.0 3.3 copy-start.9
  324.3 92.2 %all-to-all-start = ((bf16[16,7,4096]{2,1,0:T(8,128)(2,1)}), bf16[16,7,4096]{2,1,0:T(8,128)(2,1)}, u32[]{:S(2)}, u32[]{:S(2)}) async-start(bf16[16,7,4096]{2,1,0:T(8,128)(2,1)} %copy.83), calls=%async_computation.1 | async-start | bytes 2097152 | tf_op jit(solution)/shard_map/all_to_all | solution.py:143
Sparse Core Ops, SparseCore 0:
  304.6 187.5 reduce-scatter.1
